TPU v7x, 128 devices: a whole 4x4x4 slice. The times are simulated.
128 devices in a mesh: row: 8 (over z, core), col: 16 (over x, y).
Axes of the slice: x: 4, y: 4, z: 4, core: 2. Of those that a mesh axis runs over, the one named last changes fastest.
Arguments:
- tokens: bfloat16 [4096, 2048], P('col', 'row'), may hold values from -6 to 6
- router: bfloat16 [2048, 32], replicated, may hold values from -0.125 to 0.125
- shared_gate_vector: bfloat16 [2048], replicated, may hold values from -0.125 to 0.125
- shared_gate_weight: bfloat16 [2048, 5632], P('col', 'row'), may hold values from -0.125 to 0.125
- shared_up_weight: bfloat16 [2048, 5632], P('col', 'row'), may hold values from -0.125 to 0.125
- shared_down_weight: bfloat16 [5632, 2048], P('row', 'col'), may hold values from -0.078125 to 0.078125
- routed_gate_weight: bfloat16 [32, 2048, 1408], P('col', None, 'row'), may hold values from -0.125 to 0.125
- routed_up_weight: bfloat16 [32, 2048, 1408], P('col', None, 'row'), may hold values from -0.125 to 0.125
- routed_down_weight: bfloat16 [32, 1408, 2048], P('col', 'row'), may hold values from -0.15625 to 0.15625
- adapter_input_factor: bfloat16 [64, 16, 2048], P(None, None, 'row'), may hold values from -0.125 to 0.125
- adapter_output_factor: bfloat16 [64, 16, 5632], P(None, None, 'row'), may hold values from -0.29882812 to 0.29882812
- routes: int32 [4096, 4], P('col'), may hold values from 0 to 31, all different within a row; in each aligned block of 256 rows (0 to 255, 256 to 511, ...) at most 64 rows name the same one
- lengths: int32 [16, 16], P('col'), may hold values from 1 to 128, 256 in all within a row
- prompt_adapter_index: int32 [16, 16], P('col'), may hold values from 0 to 15
- active_adapter_index: int32 [16], replicated, may hold values from 0 to 63, as said below
Outputs:
- moe_out: float32 [4096, 2048], P('col', 'row')
Inputs may be any that keep to these rules, and one draw needn't show every extreme that they name: `routes`: in each group of 256 consecutive tokens no expert is named by more than 64 tokens, a bound that some block reaches. Each group's 16 lengths sum to 256; the longest is exactly 128. `active_adapter_index`: the 16 entries are distinct.
All inputs are finite; a program needn't handle non-finite values.
Results may differ from a plain program's by a relative error of at most 0.003.
Values may be sent and summed in bfloat16 or wider, within the bound.
No kernel may reach another device: no remote copies, remote signals or barrier semaphores. Data moves between devices by JAX's collectives and lax.ppermute only.
A program may use at most 128 MiB of HBM per device.

v0:
```python
import jax
import jax.numpy as jnp
from jax import lax
from jax.sharding import PartitionSpec as P

ADAPTER_SCALE = 2.0


def on_device(
    tokens,
    router,
    shared_gate_vector,
    shared_gate_weight,
    shared_up_weight,
    shared_down_weight,
    routed_gate_weight,
    routed_up_weight,
    routed_down_weight,
    adapter_input_factor,
    adapter_output_factor,
    routes,
    lengths,
    prompt_adapter_index,
    active_adapter_index,
):
    all_features = lax.all_gather(tokens, "row", axis=1, tiled=True)
    token_count = all_features.shape[0]
    full_width = all_features.shape[1]
    local_width = tokens.shape[1]
    col_count = lax.axis_size("col")
    local_experts = routed_gate_weight.shape[0]
    expert_count = local_experts * col_count
    route_count = routes.shape[1]
    capacity = 2 * token_count * route_count // expert_count
    logits = jnp.dot(all_features, router, preferred_element_type=jnp.float32)
    onehot = routes[:, :, None] == jnp.arange(expert_count, dtype=jnp.int32)[None, None, :]
    picked = jnp.sum(jnp.where(onehot, logits[:, None, :], 0.0), axis=2)
    raw_exp = jnp.exp(picked)
    gate_weights = raw_exp / jnp.sum(raw_exp, axis=1, keepdims=True)
    share = jax.nn.sigmoid(
        jnp.dot(all_features, shared_gate_vector, preferred_element_type=jnp.float32)
    )
    hit_table = jnp.any(onehot, axis=1).astype(jnp.int32)
    running_count = jnp.cumsum(hit_table, axis=0)
    slot_rank = running_count - hit_table
    route_rank = jnp.sum(jnp.where(onehot, slot_rank[:, None, :], 0), axis=2)
    row_index = routes * capacity + route_rank
    request_ends = jnp.cumsum(lengths[0])
    request_count = lengths.shape[1]
    token_position = jnp.arange(token_count, dtype=jnp.int32)
    request_of = jnp.sum(
        (token_position[:, None] >= request_ends[None, :]).astype(jnp.int32), axis=1
    )
    request_match = request_of[:, None] == jnp.arange(request_count, dtype=jnp.int32)[None, :]
    adapter_of = jnp.sum(jnp.where(request_match, prompt_adapter_index[0][None, :], 0), axis=1)
    picked_input_factor = jnp.take(adapter_input_factor, active_adapter_index, axis=0)
    rank_width = picked_input_factor.shape[1]
    reduced_rank_value = picked_input_factor.shape[0] * rank_width
    full_in = lax.all_gather(picked_input_factor, "row", axis=2, tiled=True).reshape(
        reduced_rank_value, full_width
    )
    low_rank = lax.dot_general(
        all_features, full_in, (((1,), (1,)), ((), ())), preferred_element_type=jnp.float32
    )
    owner = jnp.arange(reduced_rank_value, dtype=jnp.int32) // rank_width
    adapter_mask = adapter_of[:, None] == owner[None, :]
    low_masked = jnp.where(adapter_mask, low_rank.astype(jnp.bfloat16), jnp.zeros((), jnp.bfloat16))
    picked_output_factor = jnp.take(adapter_output_factor, active_adapter_index, axis=0).reshape(
        reduced_rank_value, adapter_output_factor.shape[2]
    )
    adapter_update = jnp.dot(low_masked, picked_output_factor, preferred_element_type=jnp.float32)
    shared_gate_value = jnp.dot(
        all_features,
        lax.all_gather(shared_gate_weight, "col", axis=0, tiled=True),
        preferred_element_type=jnp.float32,
    )
    shared_up_value = jnp.dot(
        all_features,
        lax.all_gather(shared_up_weight, "col", axis=0, tiled=True),
        preferred_element_type=jnp.float32,
    )
    shared_hidden_units = (
        jax.nn.silu(shared_gate_value) * (shared_up_value + ADAPTER_SCALE * adapter_update)
    ).astype(jnp.bfloat16)
    shared_part = jnp.dot(
        shared_hidden_units,
        lax.all_gather(shared_down_weight, "col", axis=1, tiled=True),
        preferred_element_type=jnp.float32,
    )
    shared_part = shared_part * share[:, None]
    positions = jnp.arange(capacity, dtype=jnp.int32)
    slot_token = jnp.sum(
        (running_count.T[:, None, :] <= positions[None, :, None]).astype(jnp.int32), axis=2
    )
    slot_valid = positions[None, :] < running_count[-1][:, None]
    picked_rows = jnp.take(all_features, jnp.minimum(slot_token, token_count - 1), axis=0)
    chosen = jnp.where(slot_valid[:, :, None], picked_rows, jnp.zeros((), jnp.bfloat16))
    outgoing = chosen.reshape(col_count, local_experts, capacity, full_width)
    slot_block = lax.all_to_all(outgoing, "col", split_axis=0, concat_axis=0, tiled=True)
    gate_part = jnp.einsum(
        "sexd,edf->sexf", slot_block, routed_gate_weight, preferred_element_type=jnp.float32
    )
    up_part = jnp.einsum(
        "sexd,edf->sexf", slot_block, routed_up_weight, preferred_element_type=jnp.float32
    )
    hidden = (jax.nn.silu(gate_part) * up_part).astype(jnp.bfloat16)
    partial_value = jnp.einsum(
        "sexf,efd->sexd", hidden, routed_down_weight, preferred_element_type=jnp.float32
    )
    summed, shared_sum = (
        lax.psum_scatter(partial_value, "row", scatter_dimension=3, tiled=True),
        lax.psum_scatter(shared_part, "row", scatter_dimension=1, tiled=True),
    )
    returned = lax.all_to_all(summed, "col", split_axis=0, concat_axis=0, tiled=True)
    flat_rows = returned.reshape(expert_count * capacity, local_width)
    routed_rows = jnp.take(flat_rows, row_index, axis=0)
    routed = jnp.sum(gate_weights[:, :, None] * routed_rows, axis=1)
    return routed + shared_sum


def solution(mesh):
    return jax.shard_map(
        on_device,
        mesh=mesh,
        in_specs=(
            P("col", "row"),
            P(),
            P(),
            P("col", "row"),
            P("col", "row"),
            P("row", "col"),
            P("col", None, "row"),
            P("col", None, "row"),
            P("col", "row", None),
            P(None, None, "row"),
            P(None, None, "row"),
            P("col", None),
            P("col", None),
            P("col", None),
            P(),
        ),
        out_specs=P("col", "row"),
        check_vma=False,
    )
```

profile of v0, /device:TPU:0, one launch (start us, length us, event | category | flops | bytes accessed | tf_op | source)
XLA Modules:
  0.0 487.8 jit_solution(12929686134690936716)
XLA Ops:
  6.5 0.7 all-gather.6.cloned.1.call-update
  8.0 1.6 gather_fusion.2
  10.2 0.7 broadcast_select_fusion
  15.1 20.0 %all-gather.6.cloned.1.call-done = bf16[256,2048]{1,0:T(8,128)(2,1)} async-done(((bf16[256,256]{1,0:T(8,128)(2,1)}), bf16[256,2048]{1,0:T(8,128)(2,1)}) %all-gather.6.cloned.1.call-update) | async-done | bytes 1048592 | tf_op jit(solution)/shard_map/all_gather | solution.py:26
  35.0 17.7 %gather_fusion = bf16[2048,2048]{1,0:T(8,128)(2,1)} fusion(bf16[256,2048]{1,0:T(8,128)(2,1)} %all-gather.6.cloned.1.call-done, s32[2048]{0:T(1024)S(1)} %broadcast_clamp_fusion), kind=kCustom, calls=%fused_computation | custom fusion | bytes 16785408 | tf_op jit(solution)/shard_map/jit(_take)/gather | solution.py:96
  52.7 7.5 %select_select_fusion = bf16[16,2,64,2048]{3,2,1,0:T(8,128)(2,1)} fusion(bf16[16,2,64,2048]{3,2,1,0:T(8,128)(2,1)} %bitcast.88, pred[16,2,64]{2,1,0:T(4,128)(4,1)S(1)} %get-tuple-element.9, pred[16,2,64]{2,1,0:T(4,128)(4,1)S(1)} %get-tuple-element.10), kind=kLoop, calls=%fused_computation.4 | loop fusion | flops 8388608 | bytes 16781312 | tf_op jit(solution)/shard_map/jit(_where)/select_n | solution.py:97
  60.2 7.0 %all-to-all-start = ((bf16[16,2,64,2048]{3,2,1,0:T(8,128)(2,1)}), bf16[16,2,64,2048]{3,2,1,0:T(8,128)(2,1)}, u32[]{:S(2)}, u32[]{:S(2)}) async-start(bf16[16,2,64,2048]{3,2,1,0:T(8,128)(2,1)} %select_select_fusion), calls=%async_computation | async-start | bytes 16777216 | tf_op jit(solution)/shard_map/all_to_all | solution.py:99
  67.9 152.1 %all-to-all-done = bf16[16,2,64,2048]{3,2,1,0:T(8,128)(2,1)} async-done(((bf16[16,2,64,2048]{3,2,1,0:T(8,128)(2,1)}), bf16[16,2,64,2048]{3,2,1,0:T(8,128)(2,1)}, u32[]{:S(2)}, u32[]{:S(2)}) %all-to-all-start) | async-done | bytes 8388640 | tf_op jit(solution)/shard_map/all_to_all | solution.py:99
  219.9 7.0 %fusion.2 = f32[2,16,64,176]{3,2,1,0:T(8,128)} fusion(bf16[16,2,64,2048]{3,2,1,0:T(8,128)(2,1)} %all-to-all-done, bf16[2,2048,176]{1,2,0:T(8,128)(2,1)S(1)} %copy-done.7), kind=kOutput, calls=%fused_computation.7 | convolution fusion | flops 1476395008 | bytes 11272192 | tf_op jit(solution)/shard_map/sexd,edf->sexf/dot_general | solution.py:100
  227.0 15.2 %convolution_bitcast_fusion = f32[16,2,64,2048]{3,2,0,1:T(8,128)} fusion(f32[2,16,64,176]{3,2,1,0:T(8,128)} %fusion.2, bf16[16,2,64,2048]{3,2,1,0:T(8,128)(2,1)} %all-to-all-done, bf16[2,176,2048]{2,1,0:T(8,128)(2,1)} %param.23, bf16[2,2048,176]{1,2,0:T(8,128)(2,1)} %param.22), kind=kOutput, calls=%fused_computation.9 | convolution fusion | flops 2954952704 | bytes 29491200 | tf_op jit(solution)/shard_map/sexf,efd->sexd/dot_general | solution.py:107
  244.4 1.7 fusion.20
  246.2 3.6 fusion.35
  249.8 35.6 %all-gather.10.cloned.1.call-done = bf16[2048,704]{0,1:T(8,128)(2,1)} async-done(((bf16[128,704]{0,1:T(8,128)(2,1)}), bf16[2048,704]{0,1:T(8,128)(2,1)}) %all-gather.10.cloned.1.call-update) | async-done | bytes 2883600 | tf_op jit(solution)/shard_map/all_gather | solution.py:79
  285.5 3.6 fusion.36
  289.1 48.2 %all-gather.14.cloned.1.call-done = bf16[704,2048]{1,0:T(8,128)(2,1)} async-done(((bf16[704,128]{1,0:T(8,128)(2,1)}), bf16[704,2048]{1,0:T(8,128)(2,1)}) %all-gather.14.cloned.1.call-update) | async-done | bytes 2883600 | tf_op jit(solution)/shard_map/all_gather | solution.py:87
  337.3 4.9 %convolution_multiply_fusion = f32[256,2048]{1,0:T(8,128)} fusion(bf16[704,2048]{1,0:T(8,128)(2,1)} %all-gather.14.cloned.1.call-done, f32[256,704]{0,1:T(8,128)} %fusion.36, bf16[256,256]{0,1:T(8,128)(2,1)S(1)} %fusion.20, bf16[256,704]{1,0:T(8,128)(2,1)S(1)} %bitcast_select_fusion, f32[256]{0:T(256)S(1)} %add_divide_fusion, f32[256,704]{0,1:T(8,128)} %fusion.35), kind=kOutput, calls=%fused_computation.10 | convolution fusion | flops 832438272 | bytes 6915072 | tf_op jit(solution)/shard_map/dot_general | solution.py:85
  342.2 88.8 %reduce-scatter.3.cloned.1.call-done = f32[16,2,64,256]{3,2,0,1:T(8,128)} async-done(((f32[16,2,64,2048]{3,2,0,1:T(8,128)}), f32[16,2,64,256]{3,2,0,1:T(8,128)}) %reduce-scatter.3.cloned.1.call-update) | async-done | bytes 2097168 | tf_op jit(solution)/shard_map/reduce_scatter | solution.py:111
  431.0 3.2 copy.52
  434.2 7.0 %all-to-all-start.1 = ((f32[16,2,64,256]{3,2,1,0:T(8,128)}), f32[16,2,64,256]{3,2,1,0:T(8,128)}, u32[]{:S(2)}, u32[]{:S(2)}) async-start(f32[16,2,64,256]{3,2,1,0:T(8,128)} %copy.52), calls=%async_computation.2 | async-start | bytes 4194304 | tf_op jit(solution)/shard_map/all_to_all | solution.py:114
  442.5 27.9 %all-to-all-done.1 = f32[16,2,64,256]{3,2,1,0:T(8,128)} async-done(((f32[16,2,64,256]{3,2,1,0:T(8,128)}), f32[16,2,64,256]{3,2,1,0:T(8,128)}, u32[]{:S(2)}, u32[]{:S(2)}) %all-to-all-start.1) | async-done | bytes 2097184 | tf_op jit(solution)/shard_map/all_to_all | solution.py:114
  470.3 5.1 %gather_fusion.1 = f32[1024,256]{1,0:T(8,128)S(1)} fusion(f32[2048,256]{1,0:T(8,128)} %bitcast.14, s32[1024]{0:T(1024)S(1)} %broadcast_clamp_fusion.1), kind=kCustom, calls=%fused_computation.1 | custom fusion | bytes 2101248 | tf_op jit(solution)/shard_map/jit(_take)/gather | solution.py:116
  475.4 1.3 reshape.164
  476.7 2.5 multiply_reduce_fusion
  479.2 1.7 add.77
  (75 shorter events, 9.4 us)
Async XLA Ops:
  6.5 236.6 %copy-start = (bf16[64,16,704]{2,1,0:T(8,128)(2,1)S(1)}, bf16[64,16,704]{2,1,0:T(8,128)(2,1)}, u32[]{:S(2)}) copy-start(bf16[64,16,704]{2,1,0:T(8,128)(2,1)} %param.25) | copy-start | bytes 4325380
  6.5 28.5 %all-gather.6.cloned.1.call-start = ((), (), s32[]{:S(2)}) async-start(), calls=%async_computation.4 | async-start | bytes 1179648 | tf_op jit(solution)/shard_map/all_gather | solution.py:26
  7.3 237.2 %all-gather.12.cloned.1.call-start = ((), (), s32[]{:S(2)}) async-start(), calls=%async_computation.8 | async-start | bytes 1179648 | tf_op jit(solution)/shard_map/all_gather | solution.py:59
  11.0 235.2 %all-gather.8.cloned.1.call-start = ((), (), s32[]{:S(2)}) async-start(), calls=%async_computation.6 | async-start | bytes 3063808 | tf_op jit(solution)/shard_map/all_gather | solution.py:74
  11.8 273.7 %all-gather.10.cloned.1.call-start = ((), (), s32[]{:S(2)}) async-start(), calls=%async_computation.7 | async-start | bytes 3063808 | tf_op jit(solution)/shard_map/all_gather | solution.py:79
  60.2 159.7 %copy-start.7 = (bf16[2,2048,176]{1,2,0:T(8,128)(2,1)S(1)}, bf16[2,2048,176]{1,2,0:T(8,128)(2,1)}, u32[]{:S(2)}) copy-start(bf16[2,2048,176]{1,2,0:T(8,128)(2,1)} %param.21) | copy-start | bytes 4325380
  60.2 159.7 %all-to-all-start = ((bf16[16,2,64,2048]{3,2,1,0:T(8,128)(2,1)}), bf16[16,2,64,2048]{3,2,1,0:T(8,128)(2,1)}, u32[]{:S(2)}, u32[]{:S(2)}) async-start(bf16[16,2,64,2048]{3,2,1,0:T(8,128)(2,1)} %select_select_fusion), calls=%async_computation | async-start | bytes 16777216 | tf_op jit(solution)/shard_map/all_to_all | solution.py:99
  67.2 270.1 %all-gather.14.cloned.1.call-start = ((), (), s32[]{:S(2)}) async-start(), calls=%async_computation.9 | async-start | bytes 3063808 | tf_op jit(solution)/shard_map/all_gather | solution.py:87
  67.8 363.2 %reduce-scatter.3.cloned.1.call-start = ((), (), s32[]{:S(2)}) async-start(), calls=%async_computation.5 | async-start | bytes 18874368 | tf_op jit(solution)/shard_map/reduce_scatter | solution.py:111
  242.2 0.7 copy-start.4
  242.2 0.7 copy-start.5
  242.2 1.6 copy-start.6
  242.2 1.8 copy-start.1
  242.2 237.0 %reduce-scatter.5.cloned.1.call-start = ((), (), s32[]{:S(2)}) async-start(), calls=%async_computation.10 | async-start | bytes 2359296 | tf_op jit(solution)/shard_map/reduce_scatter | solution.py:112
  434.2 7.1 %copy-start.3 = (s32[256,4]{0,1:T(4,128)S(1)}, s32[256,4]{0,1:T(4,128)}, u32[]{:S(2)}) copy-start(s32[256,4]{0,1:T(4,128)} %param.26) | copy-start | bytes 12292
  434.2 7.6 %copy-start.2 = (bf16[2048,32]{0,1:T(8,128)(2,1)S(1)}, bf16[2048,32]{0,1:T(8,128)(2,1)}, u32[]{:S(2)}) copy-start(bf16[2048,32]{0,1:T(8,128)(2,1)} %param.16) | copy-start | bytes 393220
  434.2 36.1 %all-to-all-start.1 = ((f32[16,2,64,256]{3,2,1,0:T(8,128)}), f32[16,2,64,256]{3,2,1,0:T(8,128)}, u32[]{:S(2)}, u32[]{:S(2)}) async-start(f32[16,2,64,256]{3,2,1,0:T(8,128)} %copy.52), calls=%async_computation.2 | async-start | bytes 4194304 | tf_op jit(solution)/shard_map/all_to_all | solution.py:114
Sparse Core Ops, SparseCore 0:
  9.0 25.9 all-gather.5
  36.7 24.2 all-gather.11
  63.1 155.2 all-gather.7
  220.5 64.9 all-gather.9
  287.4 49.8 all-gather.13
  339.6 91.3 reduce-scatter.2
  433.4 34.4 reduce-scatter.4
where the time goes:
time: 488 us
  waiting for transfers between devices  375 us (77%)
  matrix products  36.9 us (8%)
  local copies, waits for them, and re-layouts  31 us (6%)
  other arithmetic  16.6 us (3%)
  starting transfers between devices  14.4 us (3%)
  between operations  13.7 us (3%)
    all_to_all x1, waiting for transfers between devices, on_device(): lax.all_to_all(outgoing, 'col', split_axis=0, concat_axis=0, tiled=True)  152 us
    reduce_scatter x1, waiting for transfers between devices, on_device(): lax.psum_scatter(partial_value, 'row', scatter_dimension=3, tiled=True)  88.8 us
    all_gather x1, waiting for transfers between devices, on_device(): lax.all_gather(shared_down_weight, 'col', axis=1, tiled=True)  48.2 us
    all_gather x1, waiting for transfers between devices, on_device(): lax.all_gather(shared_up_weight, 'col', axis=0, tiled=True)  35.6 us
    all_to_all x1, waiting for transfers between devices, on_device(): lax.all_to_all(summed, 'col', split_axis=0, concat_axis=0, tiled=True)  27.9 us
    all_gather x1, waiting for transfers between devices, on_device(): all_features = lax.all_gather(tokens, 'row', axis=1, tiled=True)  20 us
    gather x1, local copies, waits for them, and re-layouts, on_device(): jnp.take(all_features, jnp.minimum(slot_token, token_count - 1), axis=0)  17.7 us
    dot_general x1, matrix products, on_device(): jnp.einsum('sexf,efd->sexd', hidden, routed_down_weight, preferred_elemen...  15.2 us
  transfers between devices with their start and end apart: 9, of which 6 were waited for; matrix products, arithmetic and copies ran while one was open for 17% of the time, Pallas kernels for 0%

commit v1 on v0

--- a/solution.py
+++ b/solution.py
@@ -4,6 +4,12 @@
 from jax.sharding import PartitionSpec as P
 
 ADAPTER_SCALE = 2.0
+
+
+def joined_along(blocks, dim):
+    lengths = list(blocks.shape[1:])
+    lengths[dim] *= blocks.shape[0]
+    return jnp.moveaxis(blocks, 0, dim).reshape(lengths)
 
 
 def on_device(
@@ -23,7 +29,19 @@
     prompt_adapter_index,
     active_adapter_index,
 ):
-    all_features = lax.all_gather(tokens, "row", axis=1, tiled=True)
+    devices = lax.axis_size("row")
+    pairs = [(i, (i + 1) % devices) for i in range(devices)]
+    back = [(b, a) for a, b in pairs]
+    lower, upper = ([], [])
+    for turn in range(devices - 1):
+        if turn % 2 == 0:
+            lower.append(lax.ppermute(lower[-1] if lower else tokens, "row", pairs))
+        else:
+            upper.append(lax.ppermute(upper[-1] if upper else tokens, "row", back))
+    blocks = jnp.stack([*lower[::-1], tokens, *upper])
+    shift = lax.axis_index("row") - len(lower)
+    blocks = blocks[(jnp.arange(devices) - shift) % devices]
+    all_features = joined_along(blocks, 1)
     token_count = all_features.shape[0]
     full_width = all_features.shape[1]
     local_width = tokens.shape[1]

time: 488 us -> 462 us (0.947)
  waiting for transfers between devices: 375 us -> 342 us
  starting transfers between devices: 14.4 us -> 23.9 us
    all_gather x1, waiting for transfers between devices: 0.02 us -> 38 us  [on_device(): lax.all_gather(shared_gate_weight, 'col', axis=0, tiled=True)]
    all_gather x1, waiting for transfers between devices: 35.6 us -> 0.02 us  [on_device(): lax.all_gather(shared_up_weight, 'col', axis=0, tiled=True)]
    all_to_all x1, waiting for transfers between devices: 152 us -> 126 us  [on_device(): lax.all_to_all(outgoing, 'col', split_axis=0, concat_axis=0, tiled=True)]
    all_gather x1 -> x0, waiting for transfers between devices: 20 us -> none  [on_device(): all_features = lax.all_gather(tokens, 'row', axis=1, tiled=True)]
    ppermute x0 -> x7, waiting for transfers between devices: none -> 12 us  [the longest x4 12 us: on_device(): lower.append(lax.ppermute(lower[-1] if lower else tokens, 'row', pairs))]
    ppermute x0 -> x7, starting transfers between devices: none -> 9.55 us  [the longest x3 9.52 us: on_device(): upper.append(lax.ppermute(upper[-1] if upper else tokens, 'row', back))]
    gather x1, local copies, waits for them, and re-layouts: 17.7 us -> 11 us  [on_device(): jnp.take(all_features, jnp.minimum(slot_token, token_count - 1), axis=0)]
  transfers between devices with their start and end apart: 9 -> 15, of which waited for: 6 -> 9; matrix products, arithmetic and copies ran while one was open for 17% -> 16% of each run, Pallas kernels for 0% -> 0%
where the time goes in v1:
time: 462 us; the launch traced here: 461 us
  waiting for transfers between devices  342 us (74%)
  matrix products  37.5 us (8%)
  local copies, waits for them, and re-layouts  27.4 us (6%)
  starting transfers between devices  23.9 us (5%)
  other arithmetic  16.7 us (4%)
  between operations  13.8 us (3%)
    all_to_all x1, waiting for transfers between devices, on_device(): lax.all_to_all(outgoing, 'col', split_axis=0, concat_axis=0, tiled=True)  126 us
    reduce_scatter x1, waiting for transfers between devices, on_device(): lax.psum_scatter(partial_value, 'row', scatter_dimension=3, tiled=True)  88.8 us
    all_gather x1, waiting for transfers between devices, on_device(): lax.all_gather(shared_down_weight, 'col', axis=1, tiled=True)  48.2 us
    all_gather x1, waiting for transfers between devices, on_device(): lax.all_gather(shared_gate_weight, 'col', axis=0, tiled=True)  38 us
    all_to_all x1, waiting for transfers between devices, on_device(): lax.all_to_all(summed, 'col', split_axis=0, concat_axis=0, tiled=True)  27.9 us
    dot_general x1, matrix products, on_device(): jnp.einsum('sexf,efd->sexd', hidden, routed_down_weight, preferred_elemen...  15.4 us
    ppermute x4, waiting for transfers between devices, on_device(): lower.append(lax.ppermute(lower[-1] if lower else tokens, 'row', pairs))  12 us
    gather x1, local copies, waits for them, and re-layouts, on_device(): jnp.take(all_features, jnp.minimum(slot_token, token_count - 1), axis=0)  11 us
  transfers between devices with their start and end apart: 15, of which 9 were waited for; matrix products, arithmetic and copies ran while one was open for 16% of the time, Pallas kernels for 0%

profile of v1, /device:TPU:0, one launch (start us, length us, event | category | flops | bytes accessed | tf_op | source)
XLA Modules:
  0.0 461.4 jit_solution(3280560956052822374)
XLA Ops:
  11.2 3.6 collective-permute-start.4
  17.7 5.5 %collective-permute-done.1 = bf16[256,256]{1,0:T(8,128)(2,1)S(1)} collective-permute-done((bf16[256,256]{1,0:T(8,128)(2,1)S(1)}, bf16[256,256]{1,0:T(8,128)(2,1)S(1)}, u32[]{:S(2)}, u32[]{:S(2)}) %collective-permute-start.1) | collective-permute-done | bytes 131104 | tf_op jit(solution)/shard_map/ppermute | solution.py:38
  23.3 3.0 collective-permute-start.5
  26.2 3.1 collective-permute-done.2
  29.3 3.0 collective-permute-start.6
  32.3 3.2 collective-permute-done.3
  38.6 11.0 %gather_fusion.1 = bf16[2048,2048]{1,0:T(8,128)(2,1)} fusion(bf16[256,2048]{1,0:T(8,128)(2,1)S(1)} %bitcast.105, s32[2048]{0:T(1024)S(1)} %broadcast_clamp_fusion), kind=kCustom, calls=%fused_computation.1 | custom fusion | bytes 16785408 | tf_op jit(solution)/shard_map/jit(_take)/gather | solution.py:114
  49.6 7.5 %select_select_fusion = bf16[16,2,64,2048]{3,2,1,0:T(8,128)(2,1)} fusion(bf16[16,2,64,2048]{3,2,1,0:T(8,128)(2,1)} %bitcast.111, pred[16,2,64]{2,1,0:T(4,128)(4,1)S(1)} %get-tuple-element.9, pred[16,2,64]{2,1,0:T(4,128)(4,1)S(1)} %get-tuple-element.10), kind=kLoop, calls=%fused_computation.5 | loop fusion | flops 8388608 | bytes 16781312 | tf_op jit(solution)/shard_map/jit(_where)/select_n | solution.py:115
  57.1 6.9 %all-to-all-start = ((bf16[16,2,64,2048]{3,2,1,0:T(8,128)(2,1)}), bf16[16,2,64,2048]{3,2,1,0:T(8,128)(2,1)}, u32[]{:S(2)}, u32[]{:S(2)}) async-start(bf16[16,2,64,2048]{3,2,1,0:T(8,128)(2,1)} %select_select_fusion), calls=%async_computation | async-start | bytes 16777216 | tf_op jit(solution)/shard_map/all_to_all | solution.py:117
  64.7 126.1 %all-to-all-done = bf16[16,2,64,2048]{3,2,1,0:T(8,128)(2,1)} async-done(((bf16[16,2,64,2048]{3,2,1,0:T(8,128)(2,1)}), bf16[16,2,64,2048]{3,2,1,0:T(8,128)(2,1)}, u32[]{:S(2)}, u32[]{:S(2)}) %all-to-all-start) | async-done | bytes 8388640 | tf_op jit(solution)/shard_map/all_to_all | solution.py:117
  190.7 7.4 %fusion.2 = f32[2,16,64,176]{3,2,1,0:T(8,128)} fusion(bf16[16,2,64,2048]{3,2,1,0:T(8,128)(2,1)} %all-to-all-done, bf16[2,2048,176]{1,2,0:T(8,128)(2,1)} %param.21), kind=kOutput, calls=%fused_computation.8 | convolution fusion | flops 1476395008 | bytes 11272192 | tf_op jit(solution)/shard_map/sexd,edf->sexf/dot_general | solution.py:118
  198.1 15.4 %convolution_bitcast_fusion = f32[16,2,64,2048]{3,2,0,1:T(8,128)} fusion(f32[2,16,64,176]{3,2,1,0:T(8,128)} %fusion.2, bf16[16,2,64,2048]{3,2,1,0:T(8,128)(2,1)} %all-to-all-done, bf16[2,176,2048]{2,1,0:T(8,128)(2,1)} %param.23, bf16[2,2048,176]{1,2,0:T(8,128)(2,1)} %param.22), kind=kOutput, calls=%fused_computation.10 | convolution fusion | flops 2954952704 | bytes 29491200 | tf_op jit(solution)/shard_map/sexf,efd->sexd/dot_general | solution.py:125
  215.8 1.7 fusion.19
  217.5 3.6 fusion.37
  221.1 38.0 %all-gather.5.cloned.1.call-done = bf16[2048,704]{0,1:T(8,128)(2,1)} async-done(((bf16[128,704]{0,1:T(8,128)(2,1)}), bf16[2048,704]{0,1:T(8,128)(2,1)}) %all-gather.5.cloned.1.call-update) | async-done | bytes 2883600 | tf_op jit(solution)/shard_map/all_gather | solution.py:92
  259.1 3.6 fusion.36
  262.7 48.2 %all-gather.11.cloned.1.call-done = bf16[704,2048]{1,0:T(8,128)(2,1)} async-done(((bf16[704,128]{1,0:T(8,128)(2,1)}), bf16[704,2048]{1,0:T(8,128)(2,1)}) %all-gather.11.cloned.1.call-update) | async-done | bytes 2883600 | tf_op jit(solution)/shard_map/all_gather | solution.py:105
  311.0 4.9 %convolution_multiply_fusion = f32[256,2048]{1,0:T(8,128)} fusion(bf16[704,2048]{1,0:T(8,128)(2,1)} %all-gather.11.cloned.1.call-done, f32[256,704]{0,1:T(8,128)} %fusion.37, bf16[256,256]{1,0:T(8,128)(2,1)S(1)} %fusion.19, bf16[256,704]{1,0:T(8,128)(2,1)S(1)} %bitcast_select_fusion, f32[256]{0:T(256)S(1)} %add_divide_fusion, f32[256,704]{0,1:T(8,128)} %fusion.36), kind=kOutput, calls=%fused_computation.11 | convolution fusion | flops 832438272 | bytes 6915072 | tf_op jit(solution)/shard_map/dot_general | solution.py:103
  315.9 88.8 %reduce-scatter.3.cloned.1.call-done = f32[16,2,64,256]{3,2,0,1:T(8,128)} async-done(((f32[16,2,64,2048]{3,2,0,1:T(8,128)}), f32[16,2,64,256]{3,2,0,1:T(8,128)}) %reduce-scatter.3.cloned.1.call-update) | async-done | bytes 2097168 | tf_op jit(solution)/shard_map/reduce_scatter | solution.py:129
  404.7 3.2 copy.56
  407.9 7.0 %all-to-all-start.1 = ((f32[16,2,64,256]{3,2,1,0:T(8,128)}), f32[16,2,64,256]{3,2,1,0:T(8,128)}, u32[]{:S(2)}, u32[]{:S(2)}) async-start(f32[16,2,64,256]{3,2,1,0:T(8,128)} %copy.56), calls=%async_computation.2 | async-start | bytes 4194304 | tf_op jit(solution)/shard_map/all_to_all | solution.py:132
  416.1 27.9 %all-to-all-done.1 = f32[16,2,64,256]{3,2,1,0:T(8,128)} async-done(((f32[16,2,64,256]{3,2,1,0:T(8,128)}), f32[16,2,64,256]{3,2,1,0:T(8,128)}, u32[]{:S(2)}, u32[]{:S(2)}) %all-to-all-start.1) | async-done | bytes 2097184 | tf_op jit(solution)/shard_map/all_to_all | solution.py:132
  444.0 5.1 %gather_fusion.2 = f32[1024,256]{1,0:T(8,128)S(1)} fusion(f32[2048,256]{1,0:T(8,128)} %bitcast.24, s32[1024]{0:T(1024)S(1)} %broadcast_clamp_fusion.1), kind=kCustom, calls=%fused_computation.2 | custom fusion | bytes 2101248 | tf_op jit(solution)/shard_map/jit(_take)/gather | solution.py:134
  450.3 2.5 multiply_reduce_fusion
  (96 shorter events, 17.6 us)
Async XLA Ops:
  6.5 207.9 %copy-start = (bf16[64,16,704]{2,1,0:T(8,128)(2,1)S(1)}, bf16[64,16,704]{2,1,0:T(8,128)(2,1)}, u32[]{:S(2)}) copy-start(bf16[64,16,704]{2,1,0:T(8,128)(2,1)} %param.25) | copy-start | bytes 4325380
  6.5 29.0 %copy-start.2 = (bf16[256,256]{1,0:T(8,128)(2,1)S(1)}, bf16[256,256]{1,0:T(8,128)(2,1)}, u32[]{:S(2)}) copy-start(bf16[256,256]{1,0:T(8,128)(2,1)} %param.15) | copy-start | bytes 393220
  6.5 209.2 %all-gather.9.cloned.1.call-start = ((), (), s32[]{:S(2)}) async-start(), calls=%async_computation.7 | async-start | bytes 1179648 | tf_op jit(solution)/shard_map/all_gather | solution.py:77
  10.4 207.1 %all-gather.7.cloned.1.call-start = ((), (), s32[]{:S(2)}) async-start(), calls=%async_computation.6 | async-start | bytes 3063808 | tf_op jit(solution)/shard_map/all_gather | solution.py:97
  11.1 248.0 %all-gather.5.cloned.1.call-start = ((), (), s32[]{:S(2)}) async-start(), calls=%async_computation.5 | async-start | bytes 3063808 | tf_op jit(solution)/shard_map/all_gather | solution.py:92
  11.2 6.5 %collective-permute-start = (bf16[256,256]{1,0:T(8,128)(2,1)}, bf16[256,256]{1,0:T(8,128)(2,1)S(1)}, u32[]{:S(2)}, u32[]{:S(2)}) collective-permute-start(bf16[256,256]{1,0:T(8,128)(2,1)} %param.15), channel_id=1, source_target_pairs={{0,16},{16,32},{32,48},{48,64},{64,80},{80,96},{96,112},{112,0},{1... | collective-permute-start | bytes 393224 | tf_op jit(solution)/shard_map/ppermute | solution.py:38
  11.2 12.1 %collective-permute-start.4 = (bf16[256,256]{1,0:T(8,128)(2,1)}, bf16[256,256]{1,0:T(8,128)(2,1)S(1)}, u32[]{:S(2)}, u32[]{:S(2)}) collective-permute-start(bf16[256,256]{1,0:T(8,128)(2,1)} %param.15), channel_id=1, source_target_pairs={{16,0},{32,16},{48,32},{64,48},{80,64},{96,80},{112,96},{0,112},{1... | collective-permute-start | bytes 393224 | tf_op jit(solution)/shard_map/ppermute | solution.py:40
  17.6 5.6 %collective-permute-start.1 = (bf16[256,256]{1,0:T(8,128)(2,1)S(1)}, bf16[256,256]{1,0:T(8,128)(2,1)S(1)}, u32[]{:S(2)}, u32[]{:S(2)}) collective-permute-start(bf16[256,256]{1,0:T(8,128)(2,1)S(1)} %collective-permute-done), channel_id=1, source_target_pairs={{0,16},{16,32},{32,48},{48,64},{64,80},{80,96},{96,112},{112,0},{1... | collective-permute-start | bytes 393224 | tf_op jit(solution)/shard_map/ppermute | solution.py:38
  23.2 6.0 %collective-permute-start.2 = (bf16[256,256]{1,0:T(8,128)(2,1)S(1)}, bf16[256,256]{1,0:T(8,128)(2,1)S(1)}, u32[]{:S(2)}, u32[]{:S(2)}) collective-permute-start(bf16[256,256]{1,0:T(8,128)(2,1)S(1)} %collective-permute-done.1), channel_id=1, source_target_pairs={{0,16},{16,32},{32,48},{48,64},{64,80},{80,96},{96,112},{112,0},{1... | collective-permute-start | bytes 393224 | tf_op jit(solution)/shard_map/ppermute | solution.py:38
  23.3 6.1 %collective-permute-start.5 = (bf16[256,256]{1,0:T(8,128)(2,1)S(1)}, bf16[256,256]{1,0:T(8,128)(2,1)S(1)}, u32[]{:S(2)}, u32[]{:S(2)}) collective-permute-start(bf16[256,256]{1,0:T(8,128)(2,1)S(1)} %collective-permute-done.4), channel_id=1, source_target_pairs={{16,0},{32,16},{48,32},{64,48},{80,64},{96,80},{112,96},{0,112},{1... | collective-permute-start | bytes 393224 | tf_op jit(solution)/shard_map/ppermute | solution.py:40
  29.3 6.2 %collective-permute-start.3 = (bf16[256,256]{1,0:T(8,128)(2,1)S(1)}, bf16[256,256]{1,0:T(8,128)(2,1)S(1)}, u32[]{:S(2)}, u32[]{:S(2)}) collective-permute-start(bf16[256,256]{1,0:T(8,128)(2,1)S(1)} %collective-permute-done.2), channel_id=1, source_target_pairs={{0,16},{16,32},{32,48},{48,64},{64,80},{80,96},{96,112},{112,0},{1... | collective-permute-start | bytes 393224 | tf_op jit(solution)/shard_map/ppermute | solution.py:38
  29.3 6.3 %collective-permute-start.6 = (bf16[256,256]{1,0:T(8,128)(2,1)S(1)}, bf16[256,256]{1,0:T(8,128)(2,1)S(1)}, u32[]{:S(2)}, u32[]{:S(2)}) collective-permute-start(bf16[256,256]{1,0:T(8,128)(2,1)S(1)} %collective-permute-done.5), channel_id=1, source_target_pairs={{16,0},{32,16},{48,32},{64,48},{80,64},{96,80},{112,96},{0,112},{1... | collective-permute-start | bytes 393224 | tf_op jit(solution)/shard_map/ppermute | solution.py:40
  57.1 133.6 %all-to-all-start = ((bf16[16,2,64,2048]{3,2,1,0:T(8,128)(2,1)}), bf16[16,2,64,2048]{3,2,1,0:T(8,128)(2,1)}, u32[]{:S(2)}, u32[]{:S(2)}) async-start(bf16[16,2,64,2048]{3,2,1,0:T(8,128)(2,1)} %select_select_fusion), calls=%async_computation | async-start | bytes 16777216 | tf_op jit(solution)/shard_map/all_to_all | solution.py:117
  64.0 246.9 %all-gather.11.cloned.1.call-start = ((), (), s32[]{:S(2)}) async-start(), calls=%async_computation.8 | async-start | bytes 3063808 | tf_op jit(solution)/shard_map/all_gather | solution.py:105
  64.6 340.1 %reduce-scatter.3.cloned.1.call-start = ((), (), s32[]{:S(2)}) async-start(), calls=%async_computation.4 | async-start | bytes 18874368 | tf_op jit(solution)/shard_map/reduce_scatter | solution.py:129
  213.5 0.7 copy-start.4
  213.5 0.7 copy-start.5
  213.5 1.6 copy-start.6
  213.6 239.3 %reduce-scatter.5.cloned.1.call-start = ((), (), s32[]{:S(2)}) async-start(), calls=%async_computation.9 | async-start | bytes 2359296 | tf_op jit(solution)/shard_map/reduce_scatter | solution.py:130
  407.9 7.1 %copy-start.3 = (s32[256,4]{0,1:T(4,128)S(1)}, s32[256,4]{0,1:T(4,128)}, u32[]{:S(2)}) copy-start(s32[256,4]{0,1:T(4,128)} %param.26) | copy-start | bytes 12292
  407.9 7.6 %copy-start.1 = (bf16[2048,32]{0,1:T(8,128)(2,1)S(1)}, bf16[2048,32]{0,1:T(8,128)(2,1)}, u32[]{:S(2)}) copy-start(bf16[2048,32]{0,1:T(8,128)(2,1)} %param.16) | copy-start | bytes 393220
  407.9 36.1 %all-to-all-start.1 = ((f32[16,2,64,256]{3,2,1,0:T(8,128)}), f32[16,2,64,256]{3,2,1,0:T(8,128)}, u32[]{:S(2)}, u32[]{:S(2)}) async-start(f32[16,2,64,256]{3,2,1,0:T(8,128)} %copy.56), calls=%async_computation.2 | async-start | bytes 4194304 | tf_op jit(solution)/shard_map/all_to_all | solution.py:132
Sparse Core Ops, SparseCore 0:
  10.5 27.2 all-gather.8
  39.9 140.6 all-gather.6
  182.7 76.3 all-gather.4
  261.1 49.8 all-gather.10
  313.3 91.3 reduce-scatter.2
  407.0 34.4 reduce-scatter.4
